TPU v7x, 512 devices: a whole 4x8x8 slice. The times are simulated.
512 devices in a mesh: dp: 32 (over y, z_lo), ctx: 16 (over z_hi, x, core).
Axes of the slice: x: 4, y: 8, z: 8 (z_hi: 2, z_lo: 4; z = z_hi * 4 + z_lo), core: 2. Of those that a mesh axis runs over, the one named last changes fastest.
Arguments:
- projected: bfloat16 [2, 32, 2048, 4096], P(None, 'dp', 'ctx'), may hold values from -6 to 6
- token_ids: int32 [32, 2048], P('dp', 'ctx'), may hold values from 0 to 511
- short_filters: float32 [2, 7, 4096], P(None, None, 'ctx'), may hold values from -2 to 2
- medium_filter: bfloat16 [128, 4096], P(None, 'ctx'), may hold values from -0.75 to 0.75
- skip_gain: float32 [4096], P('ctx'), may hold values from -3 to 3
Outputs:
- grad_projected: bfloat16 [2, 32, 2048, 4096], P(None, 'dp', 'ctx')
- grad_short: float32 [2, 7, 4096], P(None, None, 'ctx')
- grad_medium: float32 [128, 4096], P(None, 'ctx')
- grad_skip: float32 [4096], P('ctx')
All inputs are finite; a program needn't handle non-finite values.
Results may differ from a plain program's by a relative error of at most 0.024.
Values may be sent and summed in bfloat16 or wider, within the bound.
No kernel may reach another device: no remote copies, remote signals or barrier semaphores. Data moves between devices by JAX's collectives and lax.ppermute only.
A program may use at most 128 MiB of HBM per device.

v0:
```python
import jax
import jax.numpy as jnp
from jax import lax
from jax.sharding import PartitionSpec as P


def short_forward(extended, filters):
    short_len = filters.shape[1]
    length = extended.shape[1] - short_len + 1
    result = jnp.zeros((extended.shape[0], length, extended.shape[2]), jnp.float32)
    for offset in range(short_len):
        start = short_len - 1 - offset
        result = result + filters[:, offset][:, None, :] * extended[
            :, start : start + length
        ].astype(jnp.float32)
    return result


def short_backward(extended, filters):
    short_len = filters.shape[1]
    length = extended.shape[1] - short_len + 1
    result = jnp.zeros((extended.shape[0], length, extended.shape[2]), jnp.float32)
    for offset in range(short_len):
        result = result + filters[:, offset][:, None, :] * extended[
            :, offset : offset + length
        ].astype(jnp.float32)
    return result


def short_weights(grads, extended):
    short_len = extended.shape[1] - grads.shape[1] + 1
    length = grads.shape[1]
    rows = []
    for offset in range(short_len):
        start = short_len - 1 - offset
        rows.append(
            jnp.sum(
                grads.astype(jnp.float32) * extended[:, start : start + length].astype(jnp.float32),
                axis=1,
            )
        )
    return jnp.stack(rows, axis=1)


def depthwise(extended, kernel):
    result = lax.conv_general_dilated(
        extended[None],
        kernel[:, None, :],
        (1,),
        "VALID",
        dimension_numbers=("NWC", "WIO", "NWC"),
        feature_group_count=extended.shape[1],
        preferred_element_type=jnp.float32,
    )
    return result[0]


def local(projected, token_ids, short_filters, medium_filter, skip_gain):
    inputs = projected[:, 0]
    short_len = short_filters.shape[1]
    filter_len = medium_filter.shape[0]
    length = inputs.shape[1]
    groups = lax.axis_size("dp")
    shards = lax.axis_size("ctx")
    loss_weight = jnp.where((token_ids[0] >= 97) & (token_ids[0] <= 122), 0.1, 1.0).astype(
        jnp.bfloat16
    )
    weight_rows = jnp.broadcast_to(loss_weight[None, :, None], (1, length, shards))
    all_inputs, all_weight = (
        lax.all_to_all(inputs, "ctx", split_axis=2, concat_axis=1, tiled=True),
        lax.all_to_all(weight_rows, "ctx", split_axis=2, concat_axis=1, tiled=True),
    )
    weight_seq = all_weight[0, :, 0].astype(jnp.float32)
    padded_inputs = jnp.pad(all_inputs, ((0, 0), (short_len - 1, 0), (0, 0)))
    filtered = short_forward(padded_inputs, short_filters)
    product = (filtered[0] * filtered[1]).astype(jnp.bfloat16)
    padded_product = jnp.pad(product, ((filter_len - 1, 0), (0, 0)))
    mix = depthwise(padded_product, medium_filter[::-1]) + skip_gain * product.astype(jnp.float32)
    grad_mix = (weight_seq[:, None] * mix).astype(jnp.bfloat16)
    padded_later = jnp.pad(grad_mix, ((0, filter_len - 1), (0, 0)))
    back_product = depthwise(padded_later, medium_filter) + skip_gain * grad_mix.astype(jnp.float32)
    grad_key = (back_product * filtered[1]).astype(jnp.bfloat16)
    grad_value = (back_product * filtered[0]).astype(jnp.bfloat16)
    grad_filtered = jnp.stack([grad_key, grad_value])
    padded_grads = jnp.pad(grad_filtered, ((0, 0), (0, short_len - 1), (0, 0)))
    grad_channels = short_backward(padded_grads, short_filters).astype(jnp.bfloat16)
    grad_inputs = lax.all_to_all(grad_channels, "ctx", split_axis=1, concat_axis=2, tiled=True)
    grad_taps = depthwise(padded_product, grad_mix)[::-1]
    grad_gain = jnp.sum(grad_mix.astype(jnp.float32) * product.astype(jnp.float32), axis=0)
    grad_short = short_weights(grad_filtered, padded_inputs)
    grad_taps, grad_gain, grad_short = (
        lax.psum(grad_taps.astype(jnp.bfloat16), "dp").astype(jnp.float32),
        lax.psum(grad_gain.astype(jnp.bfloat16), "dp").astype(jnp.float32),
        lax.psum(grad_short.astype(jnp.bfloat16), "dp").astype(jnp.float32),
    )
    return (grad_inputs[:, None], grad_short / groups, grad_taps / groups, grad_gain / groups)


def solution(mesh):
    placed = (
        P(None, "dp", "ctx", None),
        P("dp", "ctx"),
        P(None, None, "ctx"),
        P(None, "ctx"),
        P("ctx"),
    )
    return jax.shard_map(
        local,
        mesh=mesh,
        in_specs=placed,
        out_specs=(P(None, "dp", "ctx", None), P(None, None, "ctx"), P(None, "ctx"), P("ctx")),
        check_vma=False,
    )
```

profile of v0, /device:TPU:2, one launch (start us, length us, event | category | flops | bytes accessed | tf_op | source)
XLA Modules:
  0.0 554.1 jit_solution(2337777558290786517)
XLA Ops:
  8.4 13.3 %all-to-all-start = ((bf16[1,128,16]{1,0,2:T(2,128)(2,1)}), bf16[1,128,16]{1,0,2:T(2,128)(2,1)S(1)}, u32[]{:S(2)}, u32[]{:S(2)}) async-start(bf16[1,128,16]{1,0,2:T(2,128)(2,1)} %broadcast_in_dim.36), calls=%async_computation | async-start | bytes 16384 | tf_op jit(solution)/shard_map/all_to_all | solution.py:71
  21.7 6.2 %copy.27 = bf16[2,1,128,4096]{2,0,3,1:T(2,128)(2,1)} copy(bf16[2,1,128,4096]{3,2,1,0:T(8,128)(2,1)} %param.5) | data formatting | bytes 4194304 | tf_op args[0]
  27.9 2.4 all-to-all-done
  30.3 7.4 %all-to-all-start.1 = ((bf16[2,128,4096]{1,0,2:T(2,128)(2,1)}), bf16[2,128,4096]{1,0,2:T(2,128)(2,1)S(1)}, u32[]{:S(2)}, u32[]{:S(2)}) async-start(bf16[2,128,4096]{1,0,2:T(2,128)(2,1)} %bitcast.5), calls=%async_computation.1 | async-start | bytes 4194304 | tf_op jit(solution)/shard_map/all_to_all | solution.py:70
  37.8 24.8 %all-to-all-done.1 = bf16[2,128,4096]{1,0,2:T(2,128)(2,1)S(1)} async-done(((bf16[2,128,4096]{1,0,2:T(2,128)(2,1)}), bf16[2,128,4096]{1,0,2:T(2,128)(2,1)S(1)}, u32[]{:S(2)}, u32[]{:S(2)}) %all-to-all-start.1) | async-done | bytes 2097184 | tf_op jit(solution)/shard_map/all_to_all | solution.py:70
  62.6 1.3 copy-done.2
  64.0 4.7 copy.28
  68.7 3.7 fusion.5
  74.7 47.9 %fusion.52 = f32[8,272,256]{2,0,1:T(8,128)S(1)} fusion(pred[8,272]{0,1:T(8,128)(4,1)S(1)} %copy-done.7, bf16[128,1,256]{2,0,1:T(8,128)(2,1)S(1)} %bitcast.113, bf16[8,399,256]{2,0,1:T(8,128)(2,1)S(1)} %fusion.75), kind=kOutput, calls=%fused_computation.76 | convolution fusion | flops 143163392 | bytes 3930240 | tf_op jit(solution)/shard_map/conv_general_dilated | solution.py:46
  123.3 1.3 fusion.33
  126.0 48.0 %fusion.49 = f32[8,272,256]{2,0,1:T(8,128)S(1)} fusion(pred[8,272]{0,1:T(8,128)(4,1)S(1)} %copy-done.7, bf16[128,1,256]{2,0,1:T(8,128)(2,1)S(1)} %bitcast.112, bf16[8,399,256]{2,0,1:T(8,128)(2,1)S(1)} %fusion.73), kind=kOutput, calls=%fused_computation.75 | convolution fusion | flops 143163392 | bytes 3930240 | tf_op jit(solution)/shard_map/conv_general_dilated | solution.py:46
  174.7 0.8 multiply_convert_fusion.1
  176.1 0.8 copy-done
  176.9 3.7 fusion.12
  180.5 14.2 %copy.37 = bf16[2,2048,256]{2,0,1:T(2,128)(2,1)} copy(bf16[2,2048,256]{2,1,0:T(8,128)(2,1)S(1)} %fusion.12) | data formatting | bytes 4194304 | tf_op jit(solution)/shard_map/convert_element_type | solution.py:86
  194.7 30.5 %all-to-all-start.2 = ((bf16[2,2048,256]{2,0,1:T(2,128)(2,1)}), bf16[2,2048,256]{2,0,1:T(2,128)(2,1)}, u32[]{:S(2)}, u32[]{:S(2)}) async-start(bf16[2,2048,256]{2,0,1:T(2,128)(2,1)} %copy.37), calls=%async_computation.2 | async-start | bytes 4194304 | tf_op jit(solution)/shard_map/all_to_all | solution.py:87
  225.2 28.2 %fusion.21 = bf16[1,128,256]{2,0,1:T(2,128)(2,1)S(1)} fusion(bf16[1,2175,256]{2,1,0:T(8,128)(2,1)} %copy-done.3, bf16[2048,1,256]{2,0,1:T(8,128)(2,1)} %fusion.33), kind=kOutput, calls=%fused_computation.40 | convolution fusion | flops 134217728 | bytes 2227712 | tf_op jit(solution)/shard_map/conv_general_dilated | solution.py:46
  254.2 1.9 multiply_reduce_fusion
  256.1 3.6 fusion.18
  259.9 88.6 %all-reduce.4 = (bf16[2,7,256]{2,0,1:T(2,128)(2,1)S(1)}, bf16[256]{0:T(256)(128)(2,1)S(1)}) all-reduce(bf16[2,7,256]{2,0,1:T(2,128)(2,1)S(1)} %constant_dynamic-update-slice_fusion, bf16[256]{0:T(256)(128)(2,1)S(1)} %get-tuple-element.12), channel_id=1, replica_groups=mesh['dp'=32,'ctx'=16] {'dp'}, use_global_device_ids=true, to_apply=%region_7.8 | all-reduce | flops 3840 | bytes 15360 | tf_op jit(solution)/shard_map/psum | solution.py:94
  349.7 191.0 %all-reduce.7.cloned.1.call-done = bf16[128,256]{1,0:T(8,128)(2,1)} async-done(((bf16[128,256]{1,0:T(8,128)(2,1)}), bf16[128,256]{1,0:T(8,128)(2,1)}) %all-reduce.7.cloned.1.call-update) | async-done | bytes 65552 | tf_op jit(solution)/shard_map/psum | solution.py:92
  540.7 1.5 convert_multiply_fusion.16
  542.2 2.8 copy.38
  545.0 2.3 broadcast_in_dim.41
  (49 shorter events, 9.0 us)
Async XLA Ops:
  8.4 21.8 %all-to-all-start = ((bf16[1,128,16]{1,0,2:T(2,128)(2,1)}), bf16[1,128,16]{1,0,2:T(2,128)(2,1)S(1)}, u32[]{:S(2)}, u32[]{:S(2)}) async-start(bf16[1,128,16]{1,0,2:T(2,128)(2,1)} %broadcast_in_dim.36), calls=%async_computation | async-start | bytes 16384 | tf_op jit(solution)/shard_map/all_to_all | solution.py:71
  30.3 7.4 %copy-start.4 = (bf16[128,256]{1,0:T(8,128)(2,1)S(1)}, bf16[128,256]{1,0:T(8,128)(2,1)}, u32[]{:S(2)}) copy-start(bf16[128,256]{1,0:T(8,128)(2,1)} %param.8) | copy-start | bytes 196612
  30.3 7.5 %copy-start.6 = (f32[2,7,256]{2,0,1:T(2,128)S(1)}, f32[2,7,256]{2,0,1:T(2,128)}, u32[]{:S(2)}) copy-start(f32[2,7,256]{2,0,1:T(2,128)} %param.7) | copy-start | bytes 43012
  30.3 32.4 %all-to-all-start.1 = ((bf16[2,128,4096]{1,0,2:T(2,128)(2,1)}), bf16[2,128,4096]{1,0,2:T(2,128)(2,1)S(1)}, u32[]{:S(2)}, u32[]{:S(2)}) async-start(bf16[2,128,4096]{1,0,2:T(2,128)(2,1)} %bitcast.5), calls=%async_computation.1 | async-start | bytes 4194304 | tf_op jit(solution)/shard_map/all_to_all | solution.py:70
  62.6 1.3 copy-start.2
  72.9 1.0 copy-start.3
  73.9 0.8 copy-start.7
  122.6 0.7 copy-start.5
  175.9 1.0 copy-start
  194.7 347.5 %all-to-all-start.2 = ((bf16[2,2048,256]{2,0,1:T(2,128)(2,1)}), bf16[2,2048,256]{2,0,1:T(2,128)(2,1)}, u32[]{:S(2)}, u32[]{:S(2)}) async-start(bf16[2,2048,256]{2,0,1:T(2,128)(2,1)} %copy.37), calls=%async_computation.2 | async-start | bytes 4194304 | tf_op jit(solution)/shard_map/all_to_all | solution.py:87
  225.2 315.5 %all-reduce.7.cloned.1.call-start = ((), (), s32[]{:S(2)}) async-start(), calls=%async_computation.3 | async-start | bytes 131072 | tf_op jit(solution)/shard_map/psum | solution.py:92
  254.2 1.9 copy-start.1
Sparse Core Ops, SparseCore 0:
  254.4 286.2 all-reduce.6
where the time goes:
time: 555 us; the launch traced here: 554 us
  waiting for transfers between devices  218 us (39%)
  matrix products  124 us (22%)
  blocking collectives  88.6 us (16%)
  starting transfers between devices  51.2 us (9%)
  local copies, waits for them, and re-layouts  37.7 us (7%)
  other arithmetic  20 us (4%)
  between operations  14.3 us (3%)
    psum x1, waiting for transfers between devices, local(): lax.psum(grad_taps.astype(jnp.bfloat16), 'dp').astype(jnp.float32)  191 us
    conv_general_dilated x3, matrix products, depthwise(): lax.conv_general_dilated(extended[None], kernel[:, None, :], (1,), 'VALID...  124 us
    psum x1, blocking collectives, local(): lax.psum(grad_short.astype(jnp.bfloat16), 'dp').astype(jnp.float32)  88.6 us
    all_to_all x1, starting transfers between devices, local(): lax.all_to_all(grad_channels, 'ctx', split_axis=1, concat_axis=2, tiled=T...  30.5 us
    all_to_all x1, waiting for transfers between devices, local(): lax.all_to_all(inputs, 'ctx', split_axis=2, concat_axis=1, tiled=True)  24.8 us
    convert_element_type x1, local copies, waits for them, and re-layouts, local(): short_backward(padded_grads, short_filters).astype(jnp.bfloat16)  14.2 us
    all_to_all x1, starting transfers between devices, local(): lax.all_to_all(weight_rows, 'ctx', split_axis=2, concat_axis=1, tiled=True)  13.3 us
  transfers between devices with their start and end apart: 4, of which 3 were waited for; matrix products, arithmetic and copies ran while one was open for 8% of the time, Pallas kernels for 0%

commit v1 on v0

--- a/solution.py
+++ b/solution.py
@@ -89,7 +89,7 @@
     grad_gain = jnp.sum(grad_mix.astype(jnp.float32) * product.astype(jnp.float32), axis=0)
     grad_short = short_weights(grad_filtered, padded_inputs)
     grad_taps, grad_gain, grad_short = (
-        lax.psum(grad_taps.astype(jnp.bfloat16), "dp").astype(jnp.float32),
+        jnp.sum(lax.all_gather(grad_taps.astype(jnp.bfloat16), "dp"), axis=0).astype(jnp.float32),
         lax.psum(grad_gain.astype(jnp.bfloat16), "dp").astype(jnp.float32),
         lax.psum(grad_short.astype(jnp.bfloat16), "dp").astype(jnp.float32),
     )

time: 555 us -> 406 us (0.73)
  waiting for transfers between devices: 218 us -> 27.2 us
  blocking collectives: 88.6 us -> 130 us
    psum x1 -> x0, waiting for transfers between devices: 191 us -> none  [local(): lax.psum(grad_taps.astype(jnp.bfloat16), 'dp').astype(jnp.float32)]
    psum x1, blocking collectives: 88.6 us -> 130 us  [local(): lax.psum(grad_short.astype(jnp.bfloat16), 'dp').astype(jnp.float32)]
    unnamed x24 -> x30, local copies, waits for them, and re-layouts: 9.37 us -> 11.3 us
  transfers between devices with their start and end apart: 4 -> 4, of which waited for: 3 -> 2; matrix products, arithmetic and copies ran while one was open for 8% -> 21% of each run, Pallas kernels for 0% -> 0%
where the time goes in v1:
time: 406 us; the launch traced here: 405 us
  blocking collectives  130 us (32%)
  matrix products  123 us (30%)
  starting transfers between devices  51.2 us (13%)
  local copies, waits for them, and re-layouts  39.4 us (10%)
  waiting for transfers between devices  27.2 us (7%)
  other arithmetic  20.1 us (5%)
  between operations  14.3 us (4%)
    psum x1, blocking collectives, local(): lax.psum(grad_short.astype(jnp.bfloat16), 'dp').astype(jnp.float32)  130 us
    conv_general_dilated x3, matrix products, depthwise(): lax.conv_general_dilated(extended[None], kernel[:, None, :], (1,), 'VALID...  123 us
    all_to_all x1, starting transfers between devices, local(): lax.all_to_all(grad_channels, 'ctx', split_axis=1, concat_axis=2, tiled=T...  30.5 us
    all_to_all x1, waiting for transfers between devices, local(): lax.all_to_all(inputs, 'ctx', split_axis=2, concat_axis=1, tiled=True)  24.8 us
    convert_element_type x1, local copies, waits for them, and re-layouts, local(): short_backward(padded_grads, short_filters).astype(jnp.bfloat16)  14 us
    all_to_all x1, starting transfers between devices, local(): lax.all_to_all(weight_rows, 'ctx', split_axis=2, concat_axis=1, tiled=True)  13.3 us
    unnamed x30, local copies, waits for them, and re-layouts  11.3 us
  transfers between devices with their start and end apart: 4, of which 2 were waited for; matrix products, arithmetic and copies ran while one was open for 21% of the time, Pallas kernels for 0%

profile of v1, /device:TPU:2, one launch (start us, length us, event | category | flops | bytes accessed | tf_op | source)
XLA Modules:
  0.0 405.4 jit_solution(13213112483225494466)
XLA Ops:
  8.4 13.3 %all-to-all-start = ((bf16[1,128,16]{1,0,2:T(2,128)(2,1)}), bf16[1,128,16]{1,0,2:T(2,128)(2,1)S(1)}, u32[]{:S(2)}, u32[]{:S(2)}) async-start(bf16[1,128,16]{1,0,2:T(2,128)(2,1)} %broadcast_in_dim.36), calls=%async_computation | async-start | bytes 16384 | tf_op jit(solution)/shard_map/all_to_all | solution.py:71
  21.7 6.2 %copy.27 = bf16[2,1,128,4096]{2,0,3,1:T(2,128)(2,1)} copy(bf16[2,1,128,4096]{3,2,1,0:T(8,128)(2,1)} %param.5) | data formatting | bytes 4194304 | tf_op args[0]
  27.9 2.4 all-to-all-done
  30.3 7.4 %all-to-all-start.1 = ((bf16[2,128,4096]{1,0,2:T(2,128)(2,1)}), bf16[2,128,4096]{1,0,2:T(2,128)(2,1)S(1)}, u32[]{:S(2)}, u32[]{:S(2)}) async-start(bf16[2,128,4096]{1,0,2:T(2,128)(2,1)} %bitcast.5), calls=%async_computation.1 | async-start | bytes 4194304 | tf_op jit(solution)/shard_map/all_to_all | solution.py:70
  37.9 24.8 %all-to-all-done.1 = bf16[2,128,4096]{1,0,2:T(2,128)(2,1)S(1)} async-done(((bf16[2,128,4096]{1,0,2:T(2,128)(2,1)}), bf16[2,128,4096]{1,0,2:T(2,128)(2,1)S(1)}, u32[]{:S(2)}, u32[]{:S(2)}) %all-to-all-start.1) | async-done | bytes 2097184 | tf_op jit(solution)/shard_map/all_to_all | solution.py:70
  62.6 1.3 copy-done.6
  64.0 4.7 %copy.28 = bf16[2,128,16,256]{3,1,2,0:T(8,128)(2,1)S(1)} copy(bf16[2,128,16,256]{1,0,3,2:T(2,128)(2,1)} %bitcast.109) | data formatting | bytes 4194304 | tf_op jit(solution)/shard_map/all_to_all | solution.py:70
  68.7 3.7 fusion.5
  74.2 48.0 %fusion.52 = f32[8,272,256]{2,0,1:T(8,128)S(1)} fusion(pred[8,272]{0,1:T(8,128)(4,1)S(1)} %copy-done.10, bf16[128,1,256]{2,0,1:T(8,128)(2,1)S(1)} %bitcast.115, bf16[8,399,256]{2,0,1:T(8,128)(2,1)S(1)} %fusion.75), kind=kOutput, calls=%fused_computation.76 | convolution fusion | flops 143163392 | bytes 3930240 | tf_op jit(solution)/shard_map/conv_general_dilated | solution.py:46
  123.4 0.9 copy-done.2
  124.8 26.7 %fusion.21 = bf16[1,128,256]{2,0,1:T(2,128)(2,1)S(1)} fusion(bf16[1,2175,256]{2,1,0:T(8,128)(2,1)S(1)} %pad_bitcast_fusion.1, bf16[2048,1,256]{2,0,1:T(8,128)(2,1)S(1)} %fusion.33), kind=kOutput, calls=%fused_computation.40 | convolution fusion | flops 134217728 | bytes 2227712 | tf_op jit(solution)/shard_map/conv_general_dilated | solution.py:46
  153.1 48.0 %fusion.49 = f32[8,272,256]{2,0,1:T(8,128)S(1)} fusion(pred[8,272]{0,1:T(8,128)(4,1)S(1)} %copy-done.10, bf16[128,1,256]{2,0,1:T(8,128)(2,1)S(1)} %bitcast.114, bf16[8,399,256]{2,0,1:T(8,128)(2,1)S(1)} %fusion.73), kind=kOutput, calls=%fused_computation.75 | convolution fusion | flops 143163392 | bytes 3930240 | tf_op jit(solution)/shard_map/conv_general_dilated | solution.py:46
  201.9 1.5 copy-done.1
  203.3 0.8 multiply_convert_fusion.1
  204.7 0.8 copy-done.4
  205.5 3.7 fusion.12
  209.2 14.0 %copy.37 = bf16[2,2048,256]{2,0,1:T(2,128)(2,1)} copy(bf16[2,2048,256]{2,1,0:T(8,128)(2,1)S(1)} %fusion.12) | data formatting | bytes 4194304 | tf_op jit(solution)/shard_map/convert_element_type | solution.py:86
  223.2 30.5 %all-to-all-start.2 = ((bf16[2,2048,256]{2,0,1:T(2,128)(2,1)}), bf16[2,2048,256]{2,0,1:T(2,128)(2,1)}, u32[]{:S(2)}, u32[]{:S(2)}) async-start(bf16[2,2048,256]{2,0,1:T(2,128)(2,1)} %copy.37), calls=%async_computation.2 | async-start | bytes 4194304 | tf_op jit(solution)/shard_map/all_to_all | solution.py:87
  253.7 1.9 multiply_reduce_fusion
  255.6 3.6 fusion.18
  259.3 130.4 %all-reduce.4 = (bf16[2,7,256]{2,0,1:T(2,128)(2,1)S(1)}, bf16[256]{0:T(256)(128)(2,1)S(1)}) all-reduce(bf16[2,7,256]{2,0,1:T(2,128)(2,1)S(1)} %constant_dynamic-update-slice_fusion, bf16[256]{0:T(256)(128)(2,1)S(1)} %get-tuple-element.12), channel_id=1, replica_groups=mesh['dp'=32,'ctx'=16] {'dp'}, use_global_device_ids=true, to_apply=%region_7.8 | all-reduce | flops 3840 | bytes 15360 | tf_op jit(solution)/shard_map/psum | solution.py:94
  390.9 2.8 copy.38
  393.7 2.3 broadcast_in_dim.41
  396.1 1.9 reduce_sum.91
  (56 shorter events, 9.6 us)
Async XLA Ops:
  8.4 21.8 %all-to-all-start = ((bf16[1,128,16]{1,0,2:T(2,128)(2,1)}), bf16[1,128,16]{1,0,2:T(2,128)(2,1)S(1)}, u32[]{:S(2)}, u32[]{:S(2)}) async-start(bf16[1,128,16]{1,0,2:T(2,128)(2,1)} %broadcast_in_dim.36), calls=%async_computation | async-start | bytes 16384 | tf_op jit(solution)/shard_map/all_to_all | solution.py:71
  30.3 7.4 %copy-start.7 = (bf16[128,256]{1,0:T(8,128)(2,1)S(1)}, bf16[128,256]{1,0:T(8,128)(2,1)}, u32[]{:S(2)}) copy-start(bf16[128,256]{1,0:T(8,128)(2,1)} %param.8) | copy-start | bytes 196612
  30.3 7.6 %copy-start.9 = (f32[2,7,256]{2,0,1:T(2,128)S(1)}, f32[2,7,256]{2,0,1:T(2,128)}, u32[]{:S(2)}) copy-start(f32[2,7,256]{2,0,1:T(2,128)} %param.7) | copy-start | bytes 43012
  30.3 32.4 %all-to-all-start.1 = ((bf16[2,128,4096]{1,0,2:T(2,128)(2,1)}), bf16[2,128,4096]{1,0,2:T(2,128)(2,1)S(1)}, u32[]{:S(2)}, u32[]{:S(2)}) async-start(bf16[2,128,4096]{1,0,2:T(2,128)(2,1)} %bitcast.5), calls=%async_computation.1 | async-start | bytes 4194304 | tf_op jit(solution)/shard_map/all_to_all | solution.py:70
  37.7 358.4 %all-gather.3.cloned.1.call-start = ((), (), s32[]{:S(2)}) async-start(), calls=%async_computation.3 | async-start | bytes 2162688 | tf_op jit(solution)/shard_map/all_gather | solution.py:92
  62.6 1.3 copy-start.6
  72.4 51.0 %copy-start = (f32[2,2048,256]{2,1,0:T(8,128)}, f32[2,2048,256]{2,1,0:T(8,128)S(1)}, u32[]{:S(2)}) copy-start(f32[2,2048,256]{2,1,0:T(8,128)S(1)} %fusion.5) | copy-start | bytes 12582916
  73.3 0.8 copy-start.10
  122.2 0.8 copy-start.8
  122.9 1.4 copy-start.2
  153.1 48.8 %copy-start.3 = (f32[8,272,256]{2,1,0:T(8,128)S(1)}, f32[8,272,256]{2,1,0:T(8,128)}, u32[]{:S(2)}) copy-start(f32[8,272,256]{2,1,0:T(8,128)} %copy-done.2) | copy-start | bytes 6684676
  201.1 2.2 copy-start.1
  204.5 1.0 copy-start.4
  223.2 167.7 %all-to-all-start.2 = ((bf16[2,2048,256]{2,0,1:T(2,128)(2,1)}), bf16[2,2048,256]{2,0,1:T(2,128)(2,1)}, u32[]{:S(2)}, u32[]{:S(2)}) async-start(bf16[2,2048,256]{2,0,1:T(2,128)(2,1)} %copy.37), calls=%async_computation.2 | async-start | bytes 4194304 | tf_op jit(solution)/shard_map/all_to_all | solution.py:87
  253.7 1.9 copy-start.5
Sparse Core Ops, SparseCore 0:
  152.3 200.2 all-gather.2
